TPU v7x, 128 devices: a whole 4x4x4 slice. The times are simulated.
128 devices in a mesh: dp: 4 (over z_hi, core), mp: 32 (over x, y, z_lo).
Axes of the slice: x: 4, y: 4, z: 4 (z_hi: 2, z_lo: 2; z = z_hi * 2 + z_lo), core: 2. Of those that a mesh axis runs over, the one named last changes fastest.
Arguments:
- residual_input: bfloat16 [2048, 4608], P(('dp', 'mp')), may hold values from -6 to 6
- before_attention_gain: float32 [4608], replicated, may hold values from 0.25 to 1.75
- after_attention_gain: float32 [4608], replicated, may hold values from 0.25 to 1.75
- before_feedforward_gain: float32 [4608], replicated, may hold values from 0.25 to 1.75
- after_feedforward_gain: float32 [4608], replicated, may hold values from 0.25 to 1.75
- query_weight: bfloat16 [4608, 4096], P(None, 'mp'), may hold values from -0.09375 to 0.09375
- key_value_weight: bfloat16 [4608, 2, 32, 128], P(None, None, 'mp'), as said below
- output_weight: bfloat16 [4096, 4608], P('mp'), may hold values from -0.09375 to 0.09375
- gate_matrix: bfloat16 [4608, 20480], P(None, 'mp'), may hold values from -0.09375 to 0.09375
- up_matrix: bfloat16 [4608, 20480], P(None, 'mp'), may hold values from -0.09375 to 0.09375
- down_matrix: bfloat16 [20480, 4608], P('mp'), may hold values from -0.0390625 to 0.0390625
- key_value_cache: bfloat16 [256, 2, 32, 16, 128], P('dp', None, 'mp'), as said below
- projected_lowrank_left: bfloat16 [64, 4608, 16], P('mp'), may hold values from -0.09375 to 0.09375
- projected_lowrank_right: bfloat16 [64, 16, 3, 32, 128], P(None, None, None, 'mp'), as said below
- result_lowrank_left: bfloat16 [64, 4096, 16], P(None, 'mp'), may hold values from -0.09375 to 0.09375
- result_lowrank_right: bfloat16 [64, 16, 4608], P('mp'), may hold values from -1.5 to 1.5
- token_request: int32 [4, 512], P('dp'), may hold values from 0 to 7, never falling along the last dimension, each value on 1 to 256 neighbouring positions
- lowrank_choice_by_prompt: int32 [4, 8], P('dp'), may hold values from 0 to 63
- adapter_position: int32 [64], replicated, may hold values from 0 to 63, each once
- request_pages: int32 [4, 8, 4], replicated, may hold values from 0 to 255
Outputs:
- hidden_out: bfloat16 [2048, 4608], P(('dp', 'mp'))
- kv_new: bfloat16 [2048, 2, 32, 128], P('dp', None, 'mp')
Inputs may be any that keep to these rules, and one draw needn't show every extreme that they name: `key_value_weight`: query heads h and h2 with h // 2 == h2 // 2 have equal key and value weights: they share one key and value head. `key_value_cache`: query heads that share a key and value head have equal cached keys and values. `projected_lowrank_right`: the key and value parts of query heads that share a key and value head are equal. `token_request`: numbers never fall along a group; every request has at least one token. `adapter_position`: each slot once. `request_pages`: pages may repeat within and across requests.
All inputs are finite; a program needn't handle non-finite values.
Results may differ from a plain program's by a relative error of at most 0.035.
Values may be sent and summed in bfloat16 or wider, within the bound.
No kernel may reach another device: no remote copies, remote signals or barrier semaphores. Data moves between devices by JAX's collectives and lax.ppermute only.
A program may use at most 128 MiB of HBM per device.

v0:
```python
import math
import jax
import jax.numpy as jnp
from jax import lax
from jax.sharding import PartitionSpec as P

HIDDEN_BREADTH = 4608
ASKING_CHANNELS = 32
CHANNEL_LENGTH = 128
NUM_LOW_TERMS = 64
LOW_DIMENSION = 16
SHARD_PROMPTS = 8
PPR = 4
PAGE = 16
EPS = 1e-06
SOFTCAP = 50.0
DP_AXES = ("zh", "c")
MP_AXES = ("x", "y", "zl")
MP_STAGES = (("zl",), ("x", "y"))


def gather_mp(values):
    for stage in MP_STAGES:
        values = lax.all_gather(values, stage, axis=0, tiled=True)
    return values


def scatter_mp(values):
    for stage in reversed(MP_STAGES):
        values = lax.psum_scatter(values, stage, scatter_dimension=0, tiled=True)
    return values


def sum_mp(values):
    for stage in MP_STAGES:
        values = lax.psum(values, stage)
    return values


def rms_scale(values, scaling):
    mean_square = jnp.mean(values * values, axis=-1, keepdims=True)
    return values * lax.rsqrt(mean_square + EPS) * scaling


def apply_rotary(values, token_positions):
    half_dim = values.shape[-1] // 2
    frequency = 10000.0 ** (-2.0 * jnp.arange(half_dim, dtype=jnp.float32) / values.shape[-1])
    angles = token_positions.astype(jnp.float32)[:, None] * frequency[None, :]
    cosine = jnp.cos(angles)[:, None, :]
    sine_part = jnp.sin(angles)[:, None, :]
    first_half = values[..., :half_dim]
    second_half = values[..., half_dim:]
    return jnp.concatenate(
        [
            first_half * cosine - second_half * sine_part,
            second_half * cosine + first_half * sine_part,
        ],
        axis=-1,
    )


def positions_of(segments):
    length = segments.shape[0]
    earlier = jnp.sum((segments[None, :] < segments[:, None]).astype(jnp.int32), axis=1)
    return PPR * PAGE + jnp.arange(length, dtype=jnp.int32) - earlier


def capped(scores):
    return SOFTCAP * jnp.tanh(scores / SOFTCAP)


def attend_local(query_rows, keys_new, fresh_values, keys_pre, values_pre, segments):
    scale_factor = 1.0 / math.sqrt(HIDDEN_BREADTH // ASKING_CHANNELS)
    length = segments.shape[0]
    prefix_owner = jnp.arange(keys_pre.shape[1], dtype=jnp.int32) // (PPR * PAGE)
    mask_pre = (prefix_owner[None, :] == segments[:, None])[None]
    ordinal = jnp.arange(length, dtype=jnp.int32)
    mask_new = ((segments[None, :] == segments[:, None]) & (ordinal[None, :] <= ordinal[:, None]))[
        None
    ]
    scores_pre = (
        jnp.einsum("thd,hjd->htj", query_rows, keys_pre, preferred_element_type=jnp.float32)
        * scale_factor
    )
    scores_new = (
        jnp.einsum("thd,uhd->htu", query_rows, keys_new, preferred_element_type=jnp.float32)
        * scale_factor
    )
    weight_pre = jnp.where(mask_pre, jnp.exp(capped(scores_pre)), 0.0)
    weight_new = jnp.where(mask_new, jnp.exp(capped(scores_new)), 0.0)
    totals = jnp.sum(weight_pre, axis=-1, keepdims=True) + jnp.sum(
        weight_new, axis=-1, keepdims=True
    )
    probs_pre = (weight_pre / totals).astype(jnp.bfloat16)
    probs_new = (weight_new / totals).astype(jnp.bfloat16)
    mixture = jnp.einsum("htj,hjd->thd", probs_pre, values_pre, preferred_element_type=jnp.float32)
    mixture = mixture + jnp.einsum(
        "htu,uhd->thd", probs_new, fresh_values, preferred_element_type=jnp.float32
    )
    return mixture.astype(jnp.bfloat16).reshape(length, -1)


def shards(
    residual_input,
    before_attention_gain,
    after_attention_gain,
    before_feedforward_gain,
    after_feedforward_gain,
    query_weight,
    key_value_weight,
    output_weight,
    gate_matrix,
    up_matrix,
    down_matrix,
    key_value_cache,
    projected_lowrank_left,
    projected_lowrank_right,
    result_lowrank_left,
    result_lowrank_right,
    token_request,
    lowrank_choice_by_prompt,
    adapter_position,
    request_pages,
):
    mp_index = lax.axis_index(MP_AXES)
    dp_index = lax.axis_index(DP_AXES)
    residual = residual_input.astype(jnp.float32)
    normed_rows = rms_scale(residual, before_attention_gain).astype(jnp.bfloat16)
    normalized_rows = gather_mp(normed_rows)
    prompt_ordinal = normalized_rows.shape[0]
    channel_window = query_weight.shape[1] // CHANNEL_LENGTH
    query_rows = jnp.dot(normalized_rows, query_weight, preferred_element_type=jnp.float32).reshape(
        prompt_ordinal, channel_window, CHANNEL_LENGTH
    )
    key_value_rows = jnp.dot(
        normalized_rows,
        key_value_weight.reshape(HIDDEN_BREADTH, 2 * channel_window * CHANNEL_LENGTH),
        preferred_element_type=jnp.float32,
    ).reshape(prompt_ordinal, 2, channel_window, CHANNEL_LENGTH)
    segments = token_request[0]
    request_ids = lowrank_choice_by_prompt[0]
    request_range = jnp.arange(SHARD_PROMPTS, dtype=jnp.int32)
    membership = segments[:, None] == request_range[None, :]
    adapter_range = jnp.arange(NUM_LOW_TERMS, dtype=jnp.int32)
    token_adapter = jnp.sum(jnp.where(membership, request_ids[None, :], 0), axis=1)
    token_adapter_slot = jnp.sum(
        jnp.where(token_adapter[:, None] == adapter_range[None, :], adapter_position[None, :], 0),
        axis=1,
    )
    seat_count = projected_lowrank_left.shape[0]
    local_seats = mp_index * seat_count + jnp.arange(seat_count, dtype=jnp.int32)
    seat_factors = jnp.einsum(
        "td,sdk->tsk", normalized_rows, projected_lowrank_left, preferred_element_type=jnp.float32
    )
    seat_here = token_adapter_slot[:, None] == local_seats[None, :]
    lowrank_source = jnp.sum(jnp.where(seat_here[:, :, None], seat_factors, 0.0), axis=1)
    lowrank_source = sum_mp(lowrank_source.astype(jnp.bfloat16))
    choice_mask_table = membership.astype(jnp.bfloat16)
    broadened_lines = (choice_mask_table[:, :, None] * lowrank_source[:, None, :]).reshape(
        prompt_ordinal, SHARD_PROMPTS * LOW_DIMENSION
    )
    raised_result_lines = projected_lowrank_right[request_ids].reshape(
        SHARD_PROMPTS * LOW_DIMENSION, 3 * channel_window * CHANNEL_LENGTH
    )
    adapter_query_key_value = jnp.dot(
        broadened_lines, raised_result_lines, preferred_element_type=jnp.float32
    ).reshape(prompt_ordinal, 3, channel_window, CHANNEL_LENGTH)
    token_positions = positions_of(segments)
    rotary_queries = apply_rotary(
        query_rows + adapter_query_key_value[:, 0], token_positions
    ).astype(jnp.bfloat16)
    rotary_keys = apply_rotary(
        key_value_rows[:, 0] + adapter_query_key_value[:, 1], token_positions
    ).astype(jnp.bfloat16)
    fresh_values = (key_value_rows[:, 1] + adapter_query_key_value[:, 2]).astype(jnp.bfloat16)
    kv_new = jnp.stack([rotary_keys, fresh_values], axis=1)
    own_pages = lax.dynamic_index_in_dim(request_pages, dp_index, 0, keepdims=False).reshape(
        SHARD_PROMPTS * PPR
    )
    whole_pool = lax.all_gather(key_value_cache, DP_AXES, axis=0, tiled=True)
    chosen = whole_pool[own_pages]
    keys_pre = jnp.transpose(chosen[:, 0], (1, 0, 2, 3)).reshape(
        channel_window, SHARD_PROMPTS * PPR * PAGE, CHANNEL_LENGTH
    )
    values_pre = jnp.transpose(chosen[:, 1], (1, 0, 2, 3)).reshape(
        channel_window, SHARD_PROMPTS * PPR * PAGE, CHANNEL_LENGTH
    )
    attended = attend_local(
        rotary_queries, rotary_keys, fresh_values, keys_pre, values_pre, segments
    )
    request_output_down = result_lowrank_left[request_ids]
    request_output_factors = jnp.einsum(
        "tc,rck->trk", attended, request_output_down, preferred_element_type=jnp.float32
    )
    output_adapter_piece = jnp.sum(
        jnp.where(membership[:, :, None], request_output_factors, 0.0), axis=1
    )
    result_lowrank_source = sum_mp(output_adapter_piece).astype(jnp.bfloat16)
    result_seat_lines = result_lowrank_right.shape[0]
    output_slots = mp_index * result_seat_lines + jnp.arange(result_seat_lines, dtype=jnp.int32)
    resident_here = (token_adapter_slot[:, None] == output_slots[None, :]).astype(jnp.bfloat16)
    broadened_result = (resident_here[:, :, None] * result_lowrank_source[:, None, :]).reshape(
        prompt_ordinal, result_seat_lines * LOW_DIMENSION
    )
    raised_window = result_lowrank_right.reshape(result_seat_lines * LOW_DIMENSION, HIDDEN_BREADTH)
    attn_sum = scatter_mp(
        (
            jnp.dot(attended, output_weight, preferred_element_type=jnp.float32)
            + jnp.dot(broadened_result, raised_window, preferred_element_type=jnp.float32)
        ).astype(jnp.bfloat16)
    ).astype(jnp.float32)
    after_attn = (residual + rms_scale(attn_sum, after_attention_gain)).astype(jnp.bfloat16)
    normed_ffw = rms_scale(after_attn.astype(jnp.float32), before_feedforward_gain).astype(
        jnp.bfloat16
    )
    piece = gather_mp(normed_ffw)
    gated = jnp.dot(piece, gate_matrix, preferred_element_type=jnp.float32)
    upward = jnp.dot(piece, up_matrix, preferred_element_type=jnp.float32)
    hidden = (jax.nn.gelu(gated, approximate=True) * upward).astype(jnp.bfloat16)
    ffw_sum = scatter_mp(
        jnp.dot(hidden, down_matrix, preferred_element_type=jnp.float32).astype(jnp.bfloat16)
    ).astype(jnp.float32)
    hidden_out = (
        after_attn.astype(jnp.float32) + rms_scale(ffw_sum, after_feedforward_gain)
    ).astype(jnp.bfloat16)
    return (hidden_out, kv_new)


def solution(mesh):
    fine_mesh = jax.sharding.Mesh(mesh.devices.reshape(2, 2, 4, 4, 2), DP_AXES + MP_AXES)
    return jax.shard_map(
        shards,
        mesh=fine_mesh,
        in_specs=(
            P(DP_AXES + MP_AXES, None),
            P(),
            P(),
            P(),
            P(),
            P(None, MP_AXES),
            P(None, None, MP_AXES, None),
            P(MP_AXES, None),
            P(None, MP_AXES),
            P(None, MP_AXES),
            P(MP_AXES, None),
            P(DP_AXES, None, MP_AXES, None, None),
            P(MP_AXES, None, None),
            P(None, None, None, MP_AXES, None),
            P(None, MP_AXES, None),
            P(MP_AXES, None, None),
            P(DP_AXES, None),
            P(DP_AXES, None),
            P(),
            P(),
        ),
        out_specs=(P(DP_AXES + MP_AXES, None), P(DP_AXES, None, MP_AXES, None)),
        check_vma=False,
    )
```

profile of v0, /device:TPU:1, one launch (start us, length us, event | category | flops | bytes accessed | tf_op | source)
XLA Modules:
  0.0 553.6 jit_solution(13675936725571163932)
XLA Ops:
  10.1 6.8 %all_gather.16 = bf16[32,4608]{1,0:T(8,128)(2,1)} all-gather(bf16[16,4608]{1,0:T(8,128)(2,1)S(1)} %fusion.33), channel_id=1, replica_groups=mesh['zh'=2,'c'=2,'x'=4,'y'=4,'zl'=2] {'zl'}, dimensions={0}, use_global_device_ids=true | all-gather | bytes 442368 | tf_op jit(solution)/shard_map/all_gather | solution.py:24
  18.4 2.1 gather_fusion.2
  20.5 1.7 gather_fusion.1
  23.1 2.3 copy.60
  25.4 2.5 copy.50
  31.4 8.7 %all-gather.4.cloned.1.call-done = bf16[256,2,1,16,128]{4,3,2,1,0:T(8,128)(2,1)} async-done(((bf16[64,2,1,16,128]{4,3,2,1,0:T(8,128)(2,1)}), bf16[256,2,1,16,128]{4,3,2,1,0:T(8,128)(2,1)}) %all-gather.4.cloned.1.call-update) | async-done | bytes 2097168 | tf_op jit(solution)/shard_map/all_gather | solution.py:180
  40.0 2.9 gather_fusion
  44.6 50.0 %all-gather.6.cloned.1.call-done = bf16[512,4608]{1,0:T(8,128)(2,1)} async-done(((bf16[32,4608]{1,0:T(8,128)(2,1)}), bf16[512,4608]{1,0:T(8,128)(2,1)}) %all-gather.6.cloned.1.call-update) | async-done | bytes 4718608 | tf_op jit(solution)/shard_map/all_gather | solution.py:24
  94.5 3.8 fusion.84
  98.4 6.8 %psum.28 = bf16[512,16]{0,1:T(8,128)(2,1)} all-reduce(bf16[512,16]{0,1:T(8,128)(2,1)S(1)} %select_reduce_fusion.2), channel_id=1, replica_groups=mesh['zh'=2,'c'=2,'x'=4,'y'=4,'zl'=2] {'zl'}, use_global_device_ids=true, to_apply=%region_4.5 | all-reduce | flops 8192 | bytes 32768 | tf_op jit(solution)/shard_map/psum | solution.py:36
  105.2 58.5 %psum.29 = bf16[512,16]{0,1:T(8,128)(2,1)S(1)} all-reduce(bf16[512,16]{0,1:T(8,128)(2,1)} %psum.28), channel_id=1, replica_groups=mesh['zh'=2,'c'=2,'x'=4,'y'=4,'zl'=2] {'x','y'}, use_global_device_ids=true, to_apply=%region_5.6 | all-reduce | flops 8192 | bytes 32768 | tf_op jit(solution)/shard_map/psum | solution.py:36
  165.8 3.9 fusion.19
  173.9 5.6 %psum.30 = f32[512,16]{0,1:T(8,128)S(1)} all-reduce(f32[512,16]{0,1:T(8,128)S(1)} %select_reduce_fusion), channel_id=1, replica_groups=mesh['zh'=2,'c'=2,'x'=4,'y'=4,'zl'=2] {'zl'}, use_global_device_ids=true, to_apply=%region_10.11 | all-reduce | flops 8192 | bytes 65536 | tf_op jit(solution)/shard_map/psum | solution.py:36
  179.5 55.6 %psum.31 = bf16[512,16]{0,1:T(8,128)(2,1)S(1)} all-reduce(f32[512,16]{0,1:T(8,128)S(1)} %psum.30), channel_id=1, replica_groups=mesh['zh'=2,'c'=2,'x'=4,'y'=4,'zl'=2] {'x','y'}, use_global_device_ids=true, to_apply=%region_11.12 | all-reduce | flops 8192 | bytes 49152 | tf_op jit(solution)/shard_map/psum | solution.py:36
  236.6 3.5 fusion
  240.2 105.5 %reduce-scatter.5.cloned.1.call-done = bf16[32,4608]{1,0:T(8,128)(2,1)} async-done(((bf16[512,4608]{1,0:T(8,128)(2,1)}), bf16[32,4608]{1,0:T(8,128)(2,1)}) %reduce-scatter.5.cloned.1.call-update) | async-done | bytes 294928 | tf_op jit(solution)/shard_map/reduce_scatter | solution.py:30
  345.8 17.8 %reduce-scatter.7.cloned.1.call-done = bf16[16,4608]{1,0:T(8,128)(2,1)} async-done(((bf16[32,4608]{1,0:T(8,128)(2,1)}), bf16[16,4608]{1,0:T(8,128)(2,1)}) %reduce-scatter.7.cloned.1.call-update) | async-done | bytes 147472 | tf_op jit(solution)/shard_map/reduce_scatter | solution.py:30
  365.9 5.3 all_gather.18
  371.5 55.4 %all-gather.8.cloned.1.call-done = bf16[512,4608]{1,0:T(8,128)(2,1)} async-done(((bf16[32,4608]{1,0:T(8,128)(2,1)}), bf16[512,4608]{1,0:T(8,128)(2,1)}) %all-gather.8.cloned.1.call-update) | async-done | bytes 4718608 | tf_op jit(solution)/shard_map/all_gather | solution.py:24
  427.0 7.4 %fusion.85 = f32[512,640]{1,0:T(8,128)S(1)} fusion(bf16[512,4608]{1,0:T(8,128)(2,1)} %all-gather.8.cloned.1.call-done, bf16[4608,640]{1,0:T(8,128)(2,1)} %param.28), kind=kOutput, calls=%fused_computation.141 | convolution fusion | flops 3019898880 | bytes 11927552 | tf_op jit(solution)/shard_map/dot_general | solution.py:217
  434.4 14.3 %convolution_convert_fusion = bf16[512,4608]{1,0:T(8,128)(2,1)} fusion(bf16[640,4608]{1,0:T(8,128)(2,1)} %param.30, bf16[512,4608]{1,0:T(8,128)(2,1)} %all-gather.8.cloned.1.call-done, bf16[4608,640]{1,0:T(8,128)(2,1)} %param.29, f32[512,640]{1,0:T(8,128)S(1)} %fusion.85), kind=kOutput, calls=%fused_computation.5 | convolution fusion | flops 6045433856 | bytes 22544384 | tf_op jit(solution)/shard_map/dot_general | solution.py:221
  448.8 77.2 %reduce-scatter.9.cloned.1.call-done = bf16[32,4608]{1,0:T(8,128)(2,1)} async-done(((bf16[512,4608]{1,0:T(8,128)(2,1)}), bf16[32,4608]{1,0:T(8,128)(2,1)}) %reduce-scatter.9.cloned.1.call-update) | async-done | bytes 294928 | tf_op jit(solution)/shard_map/reduce_scatter | solution.py:30
  526.9 17.1 %reduce-scatter.11.cloned.1.call-done = bf16[16,4608]{1,0:T(8,128)(2,1)} async-done(((bf16[32,4608]{1,0:T(8,128)(2,1)}), bf16[16,4608]{1,0:T(8,128)(2,1)}) %reduce-scatter.11.cloned.1.call-update) | async-done | bytes 147472 | tf_op jit(solution)/shard_map/reduce_scatter | solution.py:30
  545.1 1.7 fusion.38
  (109 shorter events, 22.6 us)
Async XLA Ops:
  7.2 229.4 %copy-start = (bf16[128,4608]{1,0:T(8,128)(2,1)S(1)}, bf16[128,4608]{1,0:T(8,128)(2,1)}, u32[]{:S(2)}) copy-start(bf16[128,4608]{1,0:T(8,128)(2,1)} %param.27) | copy-start | bytes 3538948
  7.2 32.9 %all-gather.4.cloned.1.call-start = ((), (), s32[]{:S(2)}) async-start(), calls=%async_computation.4 | async-start | bytes 2621440 | tf_op jit(solution)/shard_map/all_gather | solution.py:180
  7.9 86.6 %all-gather.6.cloned.1.call-start = ((), (), s32[]{:S(2)}) async-start(), calls=%async_computation.5 | async-start | bytes 5013504 | tf_op jit(solution)/shard_map/all_gather | solution.py:24
  16.8 328.9 %reduce-scatter.5.cloned.1.call-start = ((), (), s32[]{:S(2)}) async-start(), calls=%async_computation.6 | async-start | bytes 5013504 | tf_op jit(solution)/shard_map/reduce_scatter | solution.py:30
  23.1 6.1 %copy-start.9 = (s32[1,512]{1,0:T(1,128)S(1)}, s32[1,512]{1,0:T(1,128)}, u32[]{:S(2)}) copy-start(s32[1,512]{1,0:T(1,128)} %param.36) | copy-start | bytes 6148
  23.1 6.1 %copy-start.19 = (s32[1,8]{1,0:T(1,128)S(1)}, s32[1,8]{1,0:T(1,128)}, u32[]{:S(2)}) copy-start(s32[1,8]{1,0:T(1,128)} %param.37) | copy-start | bytes 100
  23.1 6.2 %copy-start.20 = (s32[64]{0:T(128)S(1)}, s32[64]{0:T(128)}, u32[]{:S(2)}) copy-start(s32[64]{0:T(128)} %param.38) | copy-start | bytes 772
  27.9 137.8 %copy-start.3 = (bf16[256,4608]{1,0:T(8,128)(2,1)S(1)}, bf16[256,4608]{1,0:T(8,128)(2,1)}, u32[]{:S(2)}) copy-start(bf16[256,4608]{1,0:T(8,128)(2,1)} %copy.50) | copy-start | bytes 7077892
  94.5 3.9 copy-start.17
  164.4 5.3 slice-start
  165.7 4.0 slice-start.1
  165.7 4.0 copy-start.5
  169.8 2.4 copy-start.8
  173.1 62.0 %copy-start.6 = (bf16[2,16,4608]{2,1,0:T(8,128)(2,1)S(1)}, bf16[2,16,4608]{2,1,0:T(8,128)(2,1)}, u32[]{:S(2)}) copy-start(bf16[2,16,4608]{2,1,0:T(8,128)(2,1)} %param.35) | copy-start | bytes 884740
  173.1 62.0 %copy-start.15 = (bf16[512,2]{0,1:T(2,128)(2,1)S(1)}, bf16[512,2]{0,1:T(2,128)(2,1)}, u32[]{:S(2)}) copy-start(bf16[512,2]{0,1:T(2,128)(2,1)} %get-tuple-element.14) | copy-start | bytes 6148
  240.1 124.5 %copy-start.4 = (bf16[16,4608]{1,0:T(8,128)(2,1)S(1)}, bf16[16,4608]{1,0:T(8,128)(2,1)}, u32[]{:S(2)}) copy-start(bf16[16,4608]{1,0:T(8,128)(2,1)} %param.20) | copy-start | bytes 442372
  240.1 124.5 %copy-start.11 = (f32[4608]{0:T(1024)S(1)}, f32[4608]{0:T(1024)}, u32[]{:S(2)}) copy-start(f32[4608]{0:T(1024)} %param.22) | copy-start | bytes 55300
  240.1 125.7 %copy-start.12 = (f32[4608]{0:T(1024)S(1)}, f32[4608]{0:T(1024)}, u32[]{:S(2)}) copy-start(f32[4608]{0:T(1024)} %param.23) | copy-start | bytes 55300
  240.2 123.4 %reduce-scatter.7.cloned.1.call-start = ((), (), s32[]{:S(2)}) async-start(), calls=%async_computation.7 | async-start | bytes 442368 | tf_op jit(solution)/shard_map/reduce_scatter | solution.py:30
  345.7 81.2 %all-gather.8.cloned.1.call-start = ((), (), s32[]{:S(2)}) async-start(), calls=%async_computation.8 | async-start | bytes 5013504 | tf_op jit(solution)/shard_map/all_gather | solution.py:24
  371.3 154.7 %reduce-scatter.9.cloned.1.call-start = ((), (), s32[]{:S(2)}) async-start(), calls=%async_computation.9 | async-start | bytes 5013504 | tf_op jit(solution)/shard_map/reduce_scatter | solution.py:30
  434.4 112.4 %copy-start.1 = (bf16[128,4608]{1,0:T(8,128)(2,1)S(1)}, bf16[128,4608]{1,0:T(8,128)(2,1)}, u32[]{:S(2)}) copy-start(bf16[128,4608]{1,0:T(8,128)(2,1)} %param.27) | copy-start | bytes 3538948
  448.7 96.3 %copy-start.13 = (f32[4608]{0:T(1024)S(1)}, f32[4608]{0:T(1024)}, u32[]{:S(2)}) copy-start(f32[4608]{0:T(1024)} %param.24) | copy-start | bytes 55300
  448.7 95.2 %reduce-scatter.11.cloned.1.call-start = ((), (), s32[]{:S(2)}) async-start(), calls=%async_computation.10 | async-start | bytes 442368 | tf_op jit(solution)/shard_map/reduce_scatter | solution.py:30
  (7 other events, 12.2 us)
Sparse Core Ops, SparseCore 0:
  9.7 30.3 all-gather.3
  42.2 52.2 all-gather.5
  240.3 105.3 reduce-scatter.4
  347.9 15.6 reduce-scatter.6
  371.4 55.4 all-gather.7
  448.9 77.0 reduce-scatter.8
  528.3 15.6 reduce-scatter.10
where the time goes:
time: 554 us
  waiting for transfers between devices  332 us (60%)
  blocking collectives  139 us (25%)
  matrix products  39 us (7%)
  local copies, waits for them, and re-layouts  15.9 us (3%)
  between operations  14.6 us (3%)
  other arithmetic  12.7 us (2%)
    reduce_scatter x4, waiting for transfers between devices, scatter_mp(): values = lax.psum_scatter(values, stage, scatter_dimension=0, tiled=True)  218 us
    psum x4, blocking collectives, sum_mp(): values = lax.psum(values, stage)  127 us
    all_gather x2, waiting for transfers between devices, gather_mp(): values = lax.all_gather(values, stage, axis=0, tiled=True)  105 us
    dot_general x1, matrix products, shards(): jnp.dot(hidden, down_matrix, preferred_element_type=jnp.float32)  14.3 us
    all_gather x2, blocking collectives, gather_mp(): values = lax.all_gather(values, stage, axis=0, tiled=True)  12.1 us
  transfers between devices with their start and end apart: 7, of which 7 were waited for; matrix products, arithmetic and copies ran while one was open for 4% of the time, Pallas kernels for 0%

commit v1 on v0

--- a/solution.py
+++ b/solution.py
@@ -33,7 +33,7 @@
 
 def sum_mp(values):
     for stage in MP_STAGES:
-        values = lax.psum(values, stage)
+        values = jnp.sum(lax.all_gather(values, stage), axis=0)
     return values
 
 

time: 554 us -> 457 us (0.82)
  blocking collectives: 139 us -> 53.7 us
  waiting for transfers between devices: 332 us -> 317 us
    psum x4 -> x0, blocking collectives: 127 us -> none  [sum_mp(): values = lax.psum(values, stage)]
    all_gather x0 -> x4, blocking collectives: none -> 41.6 us  [sum_mp(): values = jnp.sum(lax.all_gather(values, stage), axis=0)]
    reduce_scatter x4, waiting for transfers between devices: 218 us -> 202 us  [scatter_mp(): values = lax.psum_scatter(values, stage, scatter_dimension=0, tiled=True)]
  transfers between devices with their start and end apart: 7 -> 7, of which waited for: 7 -> 7; matrix products, arithmetic and copies ran while one was open for 4% -> 5% of each run, Pallas kernels for 0% -> 0%
where the time goes in v1:
time: 457 us; the launch traced here: 456 us
  waiting for transfers between devices  317 us (69%)
  blocking collectives  53.7 us (12%)
  matrix products  38.9 us (9%)
  local copies, waits for them, and re-layouts  17.7 us (4%)
  between operations  14.6 us (3%)
  other arithmetic  13.8 us (3%)
    reduce_scatter x4, waiting for transfers between devices, scatter_mp(): values = lax.psum_scatter(values, stage, scatter_dimension=0, tiled=True)  202 us
    all_gather x2, waiting for transfers between devices, gather_mp(): values = lax.all_gather(values, stage, axis=0, tiled=True)  105 us
    all_gather x4, blocking collectives, sum_mp(): values = jnp.sum(lax.all_gather(values, stage), axis=0)  41.6 us
    dot_general x1, matrix products, shards(): jnp.dot(hidden, down_matrix, preferred_element_type=jnp.float32)  14.3 us
    all_gather x2, blocking collectives, gather_mp(): values = lax.all_gather(values, stage, axis=0, tiled=True)  12.1 us
  transfers between devices with their start and end apart: 7, of which 7 were waited for; matrix products, arithmetic and copies ran while one was open for 5% of the time, Pallas kernels for 0%

profile of v1, /device:TPU:1, one launch (start us, length us, event | category | flops | bytes accessed | tf_op | source)
XLA Modules:
  0.0 455.9 jit_solution(11044738963353640985)
XLA Ops:
  10.1 6.8 %all_gather.38 = bf16[32,4608]{1,0:T(8,128)(2,1)} all-gather(bf16[16,4608]{1,0:T(8,128)(2,1)S(1)} %fusion.33), channel_id=1, replica_groups=mesh['zh'=2,'c'=2,'x'=4,'y'=4,'zl'=2] {'zl'}, dimensions={0}, use_global_device_ids=true | all-gather | bytes 442368 | tf_op jit(solution)/shard_map/all_gather | solution.py:24
  18.4 2.1 gather_fusion.2
  20.5 1.7 gather_fusion.1
  23.1 2.3 copy.71
  25.4 2.5 copy.59
  31.3 8.7 %all-gather.8.cloned.1.call-done = bf16[256,2,1,16,128]{4,3,2,1,0:T(8,128)(2,1)} async-done(((bf16[64,2,1,16,128]{4,3,2,1,0:T(8,128)(2,1)}), bf16[256,2,1,16,128]{4,3,2,1,0:T(8,128)(2,1)}) %all-gather.8.cloned.1.call-update) | async-done | bytes 2097168 | tf_op jit(solution)/shard_map/all_gather | solution.py:180
  40.0 2.9 gather_fusion
  44.6 50.0 %all-gather.10.cloned.1.call-done = bf16[512,4608]{1,0:T(8,128)(2,1)} async-done(((bf16[32,4608]{1,0:T(8,128)(2,1)}), bf16[512,4608]{1,0:T(8,128)(2,1)}) %all-gather.10.cloned.1.call-update) | async-done | bytes 4718608 | tf_op jit(solution)/shard_map/all_gather | solution.py:24
  94.5 3.8 fusion.84
  98.4 3.4 all-gather
  104.0 17.9 %all-gather.1 = bf16[8192,16]{0,1:T(8,128)(2,1)S(1)} all-gather(bf16[512,16]{0,1:T(8,128)(2,1)S(1)} %reduce_sum.145), channel_id=3, replica_groups=mesh['zh'=2,'c'=2,'x'=4,'y'=4,'zl'=2] {'x','y'}, dimensions={0}, use_global_device_ids=true | all-gather | bytes 278528 | tf_op jit(solution)/shard_map/all_gather | solution.py:36
  124.2 3.9 fusion.19
  132.3 3.4 all-gather.2
  135.9 16.9 %all-gather.3 = f32[8192,16]{0,1:T(8,128)S(1)} all-gather(f32[512,16]{0,1:T(8,128)S(1)} %reduce_sum.151), channel_id=5, replica_groups=mesh['zh'=2,'c'=2,'x'=4,'y'=4,'zl'=2] {'x','y'}, dimensions={0}, use_global_device_ids=true | all-gather | bytes 557056 | tf_op jit(solution)/shard_map/all_gather | solution.py:36
  154.7 3.5 fusion
  158.3 89.7 %reduce-scatter.5.cloned.1.call-done = bf16[32,4608]{1,0:T(8,128)(2,1)} async-done(((bf16[512,4608]{1,0:T(8,128)(2,1)}), bf16[32,4608]{1,0:T(8,128)(2,1)}) %reduce-scatter.5.cloned.1.call-update) | async-done | bytes 294928 | tf_op jit(solution)/shard_map/reduce_scatter | solution.py:30
  248.0 17.8 %reduce-scatter.7.cloned.1.call-done = bf16[16,4608]{1,0:T(8,128)(2,1)} async-done(((bf16[32,4608]{1,0:T(8,128)(2,1)}), bf16[16,4608]{1,0:T(8,128)(2,1)}) %reduce-scatter.7.cloned.1.call-update) | async-done | bytes 147472 | tf_op jit(solution)/shard_map/reduce_scatter | solution.py:30
  268.2 5.3 %all_gather.47 = bf16[32,4608]{1,0:T(8,128)(2,1)} all-gather(bf16[16,4608]{1,0:T(8,128)(2,1)S(1)} %fusion.37), channel_id=1, replica_groups=mesh['zh'=2,'c'=2,'x'=4,'y'=4,'zl'=2] {'zl'}, dimensions={0}, use_global_device_ids=true | all-gather | bytes 442368 | tf_op jit(solution)/shard_map/all_gather | solution.py:24
  273.7 55.4 %all-gather.12.cloned.1.call-done = bf16[512,4608]{1,0:T(8,128)(2,1)} async-done(((bf16[32,4608]{1,0:T(8,128)(2,1)}), bf16[512,4608]{1,0:T(8,128)(2,1)}) %all-gather.12.cloned.1.call-update) | async-done | bytes 4718608 | tf_op jit(solution)/shard_map/all_gather | solution.py:24
  329.2 7.4 %fusion.85 = f32[512,640]{1,0:T(8,128)S(1)} fusion(bf16[512,4608]{1,0:T(8,128)(2,1)} %all-gather.12.cloned.1.call-done, bf16[4608,640]{1,0:T(8,128)(2,1)} %param.28), kind=kOutput, calls=%fused_computation.143 | convolution fusion | flops 3019898880 | bytes 11927552 | tf_op jit(solution)/shard_map/dot_general | solution.py:217
  336.6 14.3 %convolution_convert_fusion = bf16[512,4608]{1,0:T(8,128)(2,1)} fusion(bf16[640,4608]{1,0:T(8,128)(2,1)} %param.30, bf16[512,4608]{1,0:T(8,128)(2,1)} %all-gather.12.cloned.1.call-done, bf16[4608,640]{1,0:T(8,128)(2,1)} %param.29, f32[512,640]{1,0:T(8,128)S(1)} %fusion.85), kind=kOutput, calls=%fused_computation.5 | convolution fusion | flops 6045433856 | bytes 22544384 | tf_op jit(solution)/shard_map/dot_general | solution.py:221
  351.0 77.3 %reduce-scatter.9.cloned.1.call-done = bf16[32,4608]{1,0:T(8,128)(2,1)} async-done(((bf16[512,4608]{1,0:T(8,128)(2,1)}), bf16[32,4608]{1,0:T(8,128)(2,1)}) %reduce-scatter.9.cloned.1.call-update) | async-done | bytes 294928 | tf_op jit(solution)/shard_map/reduce_scatter | solution.py:30
  429.2 17.1 %reduce-scatter.11.cloned.1.call-done = bf16[16,4608]{1,0:T(8,128)(2,1)} async-done(((bf16[32,4608]{1,0:T(8,128)(2,1)}), bf16[16,4608]{1,0:T(8,128)(2,1)}) %reduce-scatter.11.cloned.1.call-update) | async-done | bytes 147472 | tf_op jit(solution)/shard_map/reduce_scatter | solution.py:30
  447.4 1.7 fusion.38
  (115 shorter events, 25.5 us)
Async XLA Ops:
  7.2 147.5 %copy-start = (bf16[128,4608]{1,0:T(8,128)(2,1)S(1)}, bf16[128,4608]{1,0:T(8,128)(2,1)}, u32[]{:S(2)}) copy-start(bf16[128,4608]{1,0:T(8,128)(2,1)} %param.27) | copy-start | bytes 3538948
  7.2 32.9 %all-gather.8.cloned.1.call-start = ((), (), s32[]{:S(2)}) async-start(), calls=%async_computation.4 | async-start | bytes 2621440 | tf_op jit(solution)/shard_map/all_gather | solution.py:180
  7.9 86.6 %all-gather.10.cloned.1.call-start = ((), (), s32[]{:S(2)}) async-start(), calls=%async_computation.5 | async-start | bytes 5013504 | tf_op jit(solution)/shard_map/all_gather | solution.py:24
  16.8 231.1 %reduce-scatter.5.cloned.1.call-start = ((), (), s32[]{:S(2)}) async-start(), calls=%async_computation.6 | async-start | bytes 5013504 | tf_op jit(solution)/shard_map/reduce_scatter | solution.py:30
  23.1 6.0 %copy-start.9 = (s32[1,512]{1,0:T(1,128)S(1)}, s32[1,512]{1,0:T(1,128)}, u32[]{:S(2)}) copy-start(s32[1,512]{1,0:T(1,128)} %param.36) | copy-start | bytes 6148
  23.1 6.0 %copy-start.18 = (s32[1,8]{1,0:T(1,128)S(1)}, s32[1,8]{1,0:T(1,128)}, u32[]{:S(2)}) copy-start(s32[1,8]{1,0:T(1,128)} %param.37) | copy-start | bytes 100
  23.1 6.1 %copy-start.19 = (s32[64]{0:T(128)S(1)}, s32[64]{0:T(128)}, u32[]{:S(2)}) copy-start(s32[64]{0:T(128)} %param.38) | copy-start | bytes 772
  27.9 96.2 %copy-start.3 = (bf16[256,4608]{1,0:T(8,128)(2,1)S(1)}, bf16[256,4608]{1,0:T(8,128)(2,1)}, u32[]{:S(2)}) copy-start(bf16[256,4608]{1,0:T(8,128)(2,1)} %copy.59) | copy-start | bytes 7077892
  122.8 5.3 %slice-start = ((s8[4718592]{0:T(1024)(128)(4,1)}), s8[4194304]{0:T(1024)(128)(4,1)S(1)}, s32[]{:S(2)}) async-start(s8[4718592]{0:T(1024)(128)(4,1)} %bitcast.114), calls=%async_computation.11 | async-start | bytes 8388608
  124.1 4.0 slice-start.1
  124.1 4.0 copy-start.5
  128.2 2.4 copy-start.8
  128.2 2.4 copy-start.10
  131.6 21.7 %copy-start.6 = (bf16[2,16,4608]{2,1,0:T(8,128)(2,1)S(1)}, bf16[2,16,4608]{2,1,0:T(8,128)(2,1)}, u32[]{:S(2)}) copy-start(bf16[2,16,4608]{2,1,0:T(8,128)(2,1)} %param.35) | copy-start | bytes 884740
  131.6 21.7 %copy-start.15 = (bf16[512,2]{0,1:T(2,128)(2,1)S(1)}, bf16[512,2]{0,1:T(2,128)(2,1)}, u32[]{:S(2)}) copy-start(bf16[512,2]{0,1:T(2,128)(2,1)} %get-tuple-element.16) | copy-start | bytes 6148
  158.2 108.7 %copy-start.4 = (bf16[16,4608]{1,0:T(8,128)(2,1)S(1)}, bf16[16,4608]{1,0:T(8,128)(2,1)}, u32[]{:S(2)}) copy-start(bf16[16,4608]{1,0:T(8,128)(2,1)} %param.20) | copy-start | bytes 442372
  158.2 108.7 %copy-start.11 = (f32[4608]{0:T(1024)S(1)}, f32[4608]{0:T(1024)}, u32[]{:S(2)}) copy-start(f32[4608]{0:T(1024)} %param.22) | copy-start | bytes 55300
  158.2 109.9 %copy-start.12 = (f32[4608]{0:T(1024)S(1)}, f32[4608]{0:T(1024)}, u32[]{:S(2)}) copy-start(f32[4608]{0:T(1024)} %param.23) | copy-start | bytes 55300
  158.2 107.6 %reduce-scatter.7.cloned.1.call-start = ((), (), s32[]{:S(2)}) async-start(), calls=%async_computation.7 | async-start | bytes 442368 | tf_op jit(solution)/shard_map/reduce_scatter | solution.py:30
  248.0 81.2 %all-gather.12.cloned.1.call-start = ((), (), s32[]{:S(2)}) async-start(), calls=%async_computation.8 | async-start | bytes 5013504 | tf_op jit(solution)/shard_map/all_gather | solution.py:24
  273.5 154.8 %reduce-scatter.9.cloned.1.call-start = ((), (), s32[]{:S(2)}) async-start(), calls=%async_computation.9 | async-start | bytes 5013504 | tf_op jit(solution)/shard_map/reduce_scatter | solution.py:30
  336.6 112.5 %copy-start.1 = (bf16[128,4608]{1,0:T(8,128)(2,1)S(1)}, bf16[128,4608]{1,0:T(8,128)(2,1)}, u32[]{:S(2)}) copy-start(bf16[128,4608]{1,0:T(8,128)(2,1)} %param.27) | copy-start | bytes 3538948
  350.9 96.5 %copy-start.13 = (f32[4608]{0:T(1024)S(1)}, f32[4608]{0:T(1024)}, u32[]{:S(2)}) copy-start(f32[4608]{0:T(1024)} %param.24) | copy-start | bytes 55300
  350.9 95.4 %reduce-scatter.11.cloned.1.call-start = ((), (), s32[]{:S(2)}) async-start(), calls=%async_computation.10 | async-start | bytes 442368 | tf_op jit(solution)/shard_map/reduce_scatter | solution.py:30
  (6 other events, 9.8 us)
Sparse Core Ops, SparseCore 0:
  9.7 30.3 all-gather.7
  42.2 52.2 all-gather.9
  158.3 89.5 reduce-scatter.4
  250.1 15.5 reduce-scatter.6
  273.6 55.4 all-gather.11
  351.1 77.1 reduce-scatter.8
  430.6 15.6 reduce-scatter.10
